TPU v7x, 32 devices: a whole 2x2x4 slice. The times are simulated.
32 devices in a mesh: ctx: 8 (over z, y), grp: 4 (over x, core).
Axes of the slice: x: 2, y: 2, z: 4, core: 2. Of those that a mesh axis runs over, the one named last changes fastest.
Arguments:
- query: bfloat16 [1024, 12288], P('ctx', 'grp')
- land_keys: bfloat16 [32, 768], P('ctx')
- land_values: bfloat16 [32, 512], P('ctx'), may hold values from -6 to 6
- d_out: bfloat16 [1024, 8192], P('ctx', 'grp'), may hold values from -6 to 6
- doc_start: int32 [1024], P('ctx'), may hold values from 0 to 1023, as said below
Outputs:
- branch_out: bfloat16 [1024, 8192], P('ctx', 'grp')
- d_query: float32 [1024, 12288], P('ctx', 'grp')
- d_keys: float32 [32, 768], P('ctx')
- d_values: float32 [32, 512], P('ctx')
Inputs may be any that keep to these rules, and one draw needn't show every extreme that they name: doc_start never decreases from one position to the next, doc_start[t] <= t, a document starts at position 0, and one starts at the last position.
All inputs are finite; a program needn't handle non-finite values.
Results may differ from a plain program's by a relative error of at most 0.0049.
Values may be sent and summed in bfloat16 or wider, within the bound.
No kernel may reach another device: no remote copies, remote signals or barrier semaphores. Data moves between devices by JAX's collectives and lax.ppermute only.
A program may use at most 64 MiB of HBM per device.

v0:
```python
import math
import jax
import jax.numpy as jnp
from jax import lax
from jax.sharding import PartitionSpec as P

KVG = 4
DK = 192
DV = 128
BLK = 32


def shards(query, land_keys, land_values, d_out, doc_start):
    tok_rows = query.shape[0]
    head_count = query.shape[1] // DK
    nl_local = land_keys.shape[0]
    score_scale = 1.0 / math.sqrt(DK)
    group_id = lax.axis_index("grp") // (lax.axis_size("grp") // KVG)
    group_keys = lax.dynamic_slice_in_dim(land_keys, group_id * DK, DK, 1)
    group_values = lax.dynamic_slice_in_dim(land_values, group_id * DV, DV, 1)
    queries = query.reshape(tok_rows, head_count, DK)
    grads_in = d_out.reshape(tok_rows, head_count, DV)
    ctx_index = lax.axis_index("ctx")
    positions = ctx_index * tok_rows + jnp.arange(tok_rows, dtype=jnp.int32)
    keys_whole, values_whole = (
        lax.all_gather(group_keys, "ctx", axis=0, tiled=True),
        lax.all_gather(group_values, "ctx", axis=0, tiled=True),
    )
    columns = jnp.arange(keys_whole.shape[0], dtype=jnp.int32)
    allowed = (columns[None, :] * BLK >= doc_start[:, None]) & (
        (columns[None, :] + 1) * BLK <= positions[:, None] + 1
    )
    scores = (
        jnp.einsum("thd,jd->thj", queries, keys_whole, preferred_element_type=jnp.float32)
        * score_scale
    )
    masked, allowed = (jnp.where(allowed[:, None, :], scores, -1e30), allowed[:, None, :])
    peak = jnp.maximum(jnp.max(masked, axis=2), 0.0)
    expo = jnp.where(allowed, jnp.exp(masked - peak[..., None]), 0.0)
    denom = jnp.exp(-peak) + jnp.sum(expo, axis=2)
    weight = expo / denom[..., None]
    weight_b = weight.astype(jnp.bfloat16)
    context = jnp.einsum("thj,je->the", weight_b, values_whole, preferred_element_type=jnp.float32)
    branch_out = context.astype(jnp.bfloat16).reshape(tok_rows, head_count * DV)
    delta = jnp.sum(grads_in.astype(jnp.float32) * context, axis=2)
    d_weight = jnp.einsum("the,je->thj", grads_in, values_whole, preferred_element_type=jnp.float32)
    d_score_b = (weight * (d_weight - delta[..., None])).astype(jnp.bfloat16)
    d_query = (
        jnp.einsum("thj,jd->thd", d_score_b, keys_whole, preferred_element_type=jnp.float32)
        * score_scale
    ).reshape(tok_rows, head_count * DK)
    key_grad = (
        jnp.einsum("thj,thd->jd", d_score_b, queries, preferred_element_type=jnp.float32)
        * score_scale
    )
    value_grad = jnp.einsum("thj,the->je", weight_b, grads_in, preferred_element_type=jnp.float32)
    owned = lax.psum_scatter(
        jnp.concatenate([key_grad, value_grad], axis=1), "ctx", scatter_dimension=0, tiled=True
    )
    slots = (jnp.arange(KVG, dtype=jnp.int32) == group_id).astype(jnp.float32)
    placed = owned[:, None, :] * slots[None, :, None]
    totals = lax.psum(placed, "grp")
    d_keys = totals[:, :, :DK].reshape(nl_local, KVG * DK)
    d_values = totals[:, :, DK:].reshape(nl_local, KVG * DV)
    return (branch_out, d_query, d_keys, d_values)


def solution(mesh):
    return jax.shard_map(
        shards,
        mesh=mesh,
        in_specs=(P("ctx", "grp"), P("ctx", None), P("ctx", None), P("ctx", "grp"), P("ctx")),
        out_specs=(P("ctx", "grp"), P("ctx", "grp"), P("ctx", None), P("ctx", None)),
        check_vma=False,
    )
```

profile of v0, /device:TPU:0, one launch (start us, length us, event | category | flops | bytes accessed | tf_op | source)
XLA Modules:
  0.0 104.1 jit_solution(3525271043548078328)
XLA Ops:
  0.6 0.0 copy-start
  0.6 0.0 copy-start.1
  0.7 1.3 %dynamic-slice = u32[1]{0:T(128)} dynamic-slice(u32[32]{0:T(128)} %constant.50, u32[]{:T(128)S(6)} %add.60), dynamic_slice_sizes={1} | dynamic-slice | bytes 12
  2.7 0.7 dynamic-slice_bitcast_fusion.1
  3.3 0.0 copy-done
  3.3 0.1 dynamic-slice_bitcast_fusion
  3.4 0.7 compare_and_fusion
  4.2 22.3 %all-gather.1 = bf16[8,4,128]{2,1,0:T(4,128)(2,1)S(1)} all-gather(bf16[1,4,128]{2,1,0:T(4,128)(2,1)S(1)} %dynamic-slice_bitcast_fusion.1), channel_id=1, replica_groups=mesh['ctx'=8,'grp'=4] {'ctx'}, dimensions={0}, use_global_device_ids=true | all-gather | bytes 9216 | tf_op jit(solution)/shard_map/all_gather | solution.py:27
  26.5 26.1 %all-gather = bf16[8,4,192]{2,1,0:T(4,128)(2,1)S(1)} all-gather(bf16[1,4,192]{2,1,0:T(4,128)(2,1)S(1)} %dynamic-slice_bitcast_fusion), channel_id=1, replica_groups=mesh['ctx'=8,'grp'=4] {'ctx'}, dimensions={0}, use_global_device_ids=true | all-gather | bytes 13824 | tf_op jit(solution)/shard_map/all_gather | solution.py:26
  52.6 1.3 %copy.23 = bf16[128,2048]{0,1:T(8,128)(2,1)S(1)} copy(bf16[128,2048]{1,0:T(8,128)(2,1)} %param.8) | data formatting | bytes 1048576 | tf_op args[3]
  53.9 0.0 copy-done.1
  53.9 0.4 copy.22
  54.3 0.3 fusion.13
  54.6 0.1 fusion.7
  54.7 0.3 convolution_bitcast_fusion.1
  55.0 0.4 multiply_reduce_fusion
  55.3 0.2 fusion.4
  55.6 0.3 fusion.5
  55.9 0.1 pad_maximum_fusion
  56.0 33.4 %all-reduce = f32[32,320]{1,0:T(8,128)S(1)} all-reduce(f32[32,320]{1,0:T(8,128)S(1)} %pad_maximum_fusion), channel_id=2, replica_groups=mesh['ctx'=8,'grp'=4] {'ctx'}, use_global_device_ids=true, to_apply=%region_3.4.clone | all-reduce | flops 10240 | bytes 81920
  89.4 1.0 copy.26
  90.4 0.1 broadcast_multiply_fusion
  90.5 10.3 %psum.7 = f32[4,4,320]{2,1,0:T(4,128)S(1)} all-reduce(f32[4,4,320]{2,1,0:T(4,128)S(1)} %broadcast_multiply_fusion), channel_id=1, replica_groups=mesh['ctx'=8,'grp'=4] {'grp'}, use_global_device_ids=true, to_apply=%region_4.5 | all-reduce | flops 5120 | bytes 40960 | tf_op jit(solution)/shard_map/psum | solution.py:62
  100.7 0.1 slice_bitcast_fusion
  100.8 0.7 reshape.112
  101.5 0.6 copy.32
  102.1 0.4 convolution_multiply_fusion
  102.5 1.6 %copy.27 = f32[128,3072]{1,0:T(8,128)} copy(f32[128,3072]{0,1:T(8,128)S(1)} %bitcast.46) | data formatting | bytes 3145728
  (8 shorter events, 0.1 us)
Async XLA Ops:
  0.6 2.7 %copy-start = (bf16[4,768]{1,0:T(4,128)(2,1)S(1)}, bf16[4,768]{1,0:T(4,128)(2,1)}, u32[]{:S(2)}) copy-start(bf16[4,768]{1,0:T(4,128)(2,1)} %param.6) | copy-start | bytes 18436
  0.6 53.3 %copy-start.1 = (bf16[128,3072]{1,0:T(8,128)(2,1)S(1)}, bf16[128,3072]{1,0:T(8,128)(2,1)}, u32[]{:S(2)}) copy-start(bf16[128,3072]{1,0:T(8,128)(2,1)} %param.5) | copy-start | bytes 2359300
where the time goes:
time: 104 us
  blocking collectives  92 us (88%)
  local copies, waits for them, and re-layouts  7.81 us (8%)
  matrix products  1.87 us (2%)
  between operations  1.44 us (1%)
    unnamed x1, blocking collectives  33.4 us
    all_gather x1, blocking collectives, shards(): lax.all_gather(group_keys, 'ctx', axis=0, tiled=True)  26.1 us
    all_gather x1, blocking collectives, shards(): lax.all_gather(group_values, 'ctx', axis=0, tiled=True)  22.3 us
    psum x1, blocking collectives, shards(): totals = lax.psum(placed, 'grp')  10.3 us
    unnamed x15, local copies, waits for them, and re-layouts  7.12 us

commit v1 on v0

--- a/solution.py
+++ b/solution.py
@@ -23,7 +23,9 @@
     ctx_index = lax.axis_index("ctx")
     positions = ctx_index * tok_rows + jnp.arange(tok_rows, dtype=jnp.int32)
     keys_whole, values_whole = (
-        lax.all_gather(group_keys, "ctx", axis=0, tiled=True),
+        jnp.concatenate(
+            lax.all_to_all(jnp.stack([group_keys] * lax.axis_size("ctx")), "ctx", 0, 0), axis=0
+        ),
         lax.all_gather(group_values, "ctx", axis=0, tiled=True),
     )
     columns = jnp.arange(keys_whole.shape[0], dtype=jnp.int32)

time: 104 us -> 85 us (0.82)
  blocking collectives: 92 us -> 64.7 us
  starting transfers between devices: 0 us -> 7.31 us
    all_gather x1 -> x0, blocking collectives: 26.1 us -> none  [shards(): lax.all_gather(group_keys, 'ctx', axis=0, tiled=True)]
    all_to_all x0 -> x1, starting transfers between devices: none -> 7.31 us  [shards(): lax.all_to_all(jnp.stack([group_keys] * lax.axis_size('ctx')), 'ctx', 0, 0)]
    all_gather x1, blocking collectives: 22.3 us -> 21 us  [shards(): lax.all_gather(group_values, 'ctx', axis=0, tiled=True)]
  transfers between devices with their start and end apart: 0 -> 1, of which waited for: 0 -> 0; matrix products, arithmetic and copies ran while one was open for 0% -> 4% of each run, Pallas kernels for 0% -> 0%
where the time goes in v1:
time: 85 us; the launch traced here: 84.6 us
  blocking collectives  64.7 us (76%)
  local copies, waits for them, and re-layouts  8.35 us (10%)
  starting transfers between devices  7.31 us (9%)
  matrix products  1.86 us (2%)
  between operations  1.47 us (2%)
  other arithmetic  0.97 us (1%)
    unnamed x1, blocking collectives  33.4 us
    all_gather x1, blocking collectives, shards(): lax.all_gather(group_values, 'ctx', axis=0, tiled=True)  21 us
    psum x1, blocking collectives, shards(): totals = lax.psum(placed, 'grp')  10.3 us
    all_to_all x1, starting transfers between devices, shards(): lax.all_to_all(jnp.stack([group_keys] * lax.axis_size('ctx')), 'ctx', 0, 0)  7.31 us
    unnamed x15, local copies, waits for them, and re-layouts  6.95 us
  transfers between devices with their start and end apart: 1, of which 0 were waited for; matrix products, arithmetic and copies ran while one was open for 4% of the time, Pallas kernels for 0%

profile of v1, /device:TPU:0, one launch (start us, length us, event | category | flops | bytes accessed | tf_op | source)
XLA Modules:
  0.0 84.6 jit_solution(2391531632086061814)
XLA Ops:
  0.6 0.0 copy-start
  0.6 0.0 copy-start.2
  0.7 0.0 copy-start.1
  0.7 0.7 copy-done
  1.3 0.1 constant_dynamic-slice_fusion.1
  1.4 0.6 stack.2
  2.0 7.3 %all-to-all-start = ((bf16[8,4,192]{2,1,0:T(4,128)(2,1)}), bf16[8,4,192]{2,1,0:T(4,128)(2,1)S(1)}, u32[]{:S(2)}, u32[]{:S(2)}) async-start(bf16[8,4,192]{2,1,0:T(4,128)(2,1)} %stack.2), calls=%async_computation | async-start | bytes 32768 | tf_op jit(solution)/shard_map/all_to_all | solution.py:27
  9.4 0.7 dynamic-slice_bitcast_fusion
  10.0 0.7 compare_and_fusion
  10.8 1.3 %copy.23 = bf16[128,2048]{0,1:T(8,128)(2,1)S(1)} copy(bf16[128,2048]{1,0:T(8,128)(2,1)} %param.8) | data formatting | bytes 1048576 | tf_op args[3]
  12.1 0.0 copy-done.1
  12.1 0.4 copy.22
  12.5 0.0 copy-done.2
  12.5 0.6 dynamic-slice
  13.8 21.0 %all-gather = bf16[8,4,128]{2,1,0:T(4,128)(2,1)S(1)} all-gather(bf16[1,4,128]{2,1,0:T(4,128)(2,1)S(1)} %dynamic-slice_bitcast_fusion), channel_id=1, replica_groups=mesh['ctx'=8,'grp'=4] {'ctx'}, dimensions={0}, use_global_device_ids=true | all-gather | bytes 9216 | tf_op jit(solution)/shard_map/all_gather | solution.py:29
  34.7 0.0 all-to-all-done
  34.8 0.3 fusion.13
  35.1 0.1 fusion.7
  35.1 0.3 convolution_bitcast_fusion.1
  35.4 0.4 multiply_reduce_fusion
  35.8 0.2 fusion.4
  36.0 0.3 fusion.5
  36.4 0.1 pad_maximum_fusion
  36.5 33.4 %all-reduce = f32[32,320]{1,0:T(8,128)S(1)} all-reduce(f32[32,320]{1,0:T(8,128)S(1)} %pad_maximum_fusion), channel_id=2, replica_groups=mesh['ctx'=8,'grp'=4] {'ctx'}, use_global_device_ids=true, to_apply=%region_3.4.clone | all-reduce | flops 10240 | bytes 81920
  69.9 0.1 broadcast_multiply_fusion
  70.0 10.3 %psum.7 = f32[4,4,320]{2,1,0:T(4,128)S(1)} all-reduce(f32[4,4,320]{2,1,0:T(4,128)S(1)} %broadcast_multiply_fusion), channel_id=1, replica_groups=mesh['ctx'=8,'grp'=4] {'grp'}, use_global_device_ids=true, to_apply=%region_4.5 | all-reduce | flops 5120 | bytes 40960 | tf_op jit(solution)/shard_map/psum | solution.py:64
  80.2 0.1 slice_bitcast_fusion
  80.3 0.4 convolution_multiply_fusion
  80.7 1.0 %copy.26 = bf16[128,2048]{1,0:T(8,128)(2,1)} copy(bf16[128,2048]{0,1:T(8,128)(2,1)S(1)} %bitcast.47) | data formatting | bytes 1048576
  81.7 0.7 reshape.118
  82.4 0.6 copy.32
  83.0 1.6 %copy.27 = f32[128,3072]{1,0:T(8,128)} copy(f32[128,3072]{0,1:T(8,128)S(1)} %bitcast.44) | data formatting | bytes 3145728
  (8 shorter events, 0.1 us)
Async XLA Ops:
  0.6 0.7 copy-start
  0.6 11.9 %copy-start.2 = (u32[32]{0:T(128)S(1)}, u32[32]{0:T(128)}, u32[]{:S(2)}) copy-start(u32[32]{0:T(128)} %constant.50) | copy-start | bytes 388
  0.7 11.5 %copy-start.1 = (bf16[128,3072]{1,0:T(8,128)(2,1)S(1)}, bf16[128,3072]{1,0:T(8,128)(2,1)}, u32[]{:S(2)}) copy-start(bf16[128,3072]{1,0:T(8,128)(2,1)} %param.5) | copy-start | bytes 2359300
  2.0 32.7 %all-to-all-start = ((bf16[8,4,192]{2,1,0:T(4,128)(2,1)}), bf16[8,4,192]{2,1,0:T(4,128)(2,1)S(1)}, u32[]{:S(2)}, u32[]{:S(2)}) async-start(bf16[8,4,192]{2,1,0:T(4,128)(2,1)} %stack.2), calls=%async_computation | async-start | bytes 32768 | tf_op jit(solution)/shard_map/all_to_all | solution.py:27

commit v2 on v0

--- a/solution.py
+++ b/solution.py
@@ -59,7 +59,9 @@
     )
     slots = (jnp.arange(KVG, dtype=jnp.int32) == group_id).astype(jnp.float32)
     placed = owned[:, None, :] * slots[None, :, None]
-    totals = lax.psum(placed, "grp")
+    totals = placed
+    for hop in (1, 2):
+        totals = totals + lax.ppermute(totals, "grp", [(dev, dev ^ hop) for dev in range(4)])
     d_keys = totals[:, :, :DK].reshape(nl_local, KVG * DK)
     d_values = totals[:, :, DK:].reshape(nl_local, KVG * DV)
     return (branch_out, d_query, d_keys, d_values)

time: 104 us -> 95.7 us (0.920)
  blocking collectives: 92 us -> 81.8 us
  starting transfers between devices: 0 us -> 1.52 us
  waiting for transfers between devices: 0 us -> 1.18 us
    psum x1 -> x0, blocking collectives: 10.3 us -> none  [shards(): totals = lax.psum(placed, 'grp')]
    ppermute x0 -> x2, starting transfers between devices: none -> 1.52 us  [shards(): lax.ppermute(totals, 'grp', [(dev, dev ^ hop) for dev in range(4)])]
    ppermute x0 -> x2, waiting for transfers between devices: none -> 1.18 us  [shards(): lax.ppermute(totals, 'grp', [(dev, dev ^ hop) for dev in range(4)])]
    unnamed x15 -> x19, local copies, waits for them, and re-layouts: 7.12 us -> 6.46 us
  transfers between devices with their start and end apart: 0 -> 2, of which waited for: 0 -> 1; matrix products, arithmetic and copies ran while one was open for 0% -> 3% of each run, Pallas kernels for 0% -> 0%
where the time goes in v2:
time: 95.7 us; the launch traced here: 95.5 us
  blocking collectives  81.8 us (85%)
  local copies, waits for them, and re-layouts  7.15 us (7%)
  matrix products  1.86 us (2%)
  starting transfers between devices  1.52 us (2%)
  between operations  1.51 us (2%)
  waiting for transfers between devices  1.18 us (1%)
    unnamed x1, blocking collectives  33.4 us
    all_gather x1, blocking collectives, shards(): lax.all_gather(group_keys, 'ctx', axis=0, tiled=True)  26.1 us
    all_gather x1, blocking collectives, shards(): lax.all_gather(group_values, 'ctx', axis=0, tiled=True)  22.3 us
    unnamed x19, local copies, waits for them, and re-layouts  6.46 us
  transfers between devices with their start and end apart: 2, of which 1 were waited for; matrix products, arithmetic and copies ran while one was open for 3% of the time, Pallas kernels for 0%

profile of v2, /device:TPU:0, one launch (start us, length us, event | category | flops | bytes accessed | tf_op | source)
XLA Modules:
  0.0 95.5 jit_solution(7740602941243683399)
XLA Ops:
  0.6 0.0 copy-start
  0.6 0.0 copy-start.1
  0.7 0.0 copy-start.2
  0.7 0.7 dynamic-slice_bitcast_fusion.1
  1.5 22.3 %all-gather.1 = bf16[8,4,128]{2,1,0:T(4,128)(2,1)S(1)} all-gather(bf16[1,4,128]{2,1,0:T(4,128)(2,1)S(1)} %dynamic-slice_bitcast_fusion.1), channel_id=1, replica_groups=mesh['ctx'=8,'grp'=4] {'ctx'}, dimensions={0}, use_global_device_ids=true | all-gather | bytes 9216 | tf_op jit(solution)/shard_map/all_gather | solution.py:27
  23.8 0.0 copy-done
  23.8 0.1 dynamic-slice_bitcast_fusion
  23.9 26.1 %all-gather = bf16[8,4,192]{2,1,0:T(4,128)(2,1)S(1)} all-gather(bf16[1,4,192]{2,1,0:T(4,128)(2,1)S(1)} %dynamic-slice_bitcast_fusion), channel_id=1, replica_groups=mesh['ctx'=8,'grp'=4] {'ctx'}, dimensions={0}, use_global_device_ids=true | all-gather | bytes 13824 | tf_op jit(solution)/shard_map/all_gather | solution.py:26
  50.0 1.3 %copy.23 = bf16[128,2048]{0,1:T(8,128)(2,1)S(1)} copy(bf16[128,2048]{1,0:T(8,128)(2,1)} %param.8) | data formatting | bytes 1048576 | tf_op args[3]
  51.3 0.0 copy-done.1
  51.3 0.4 copy.22
  51.7 0.0 copy-done.2
  51.7 0.1 compare_and_fusion
  51.8 0.3 fusion.14
  52.1 0.1 fusion.7
  52.2 0.3 convolution_bitcast_fusion.1
  52.4 0.4 multiply_reduce_fusion
  52.8 0.0 copy-start.3
  52.8 0.2 fusion.4
  53.0 0.3 fusion.5
  53.4 0.1 pad_maximum_fusion
  53.5 33.4 %all-reduce = f32[32,320]{1,0:T(8,128)S(1)} all-reduce(f32[32,320]{1,0:T(8,128)S(1)} %pad_maximum_fusion), channel_id=2, replica_groups=mesh['ctx'=8,'grp'=4] {'ctx'}, use_global_device_ids=true, to_apply=%region_3.4.clone | all-reduce | flops 10240 | bytes 81920
  86.9 0.0 copy-done.3
  86.9 0.6 dynamic-slice
  88.1 0.1 broadcast_multiply_fusion
  88.2 0.0 collective-permute-start
  88.2 1.2 %collective-permute-done = f32[4,4,320]{2,1,0:T(4,128)S(1)} collective-permute-done((f32[4,4,320]{2,1,0:T(4,128)S(1)}, f32[4,4,320]{2,1,0:T(4,128)S(1)}, u32[]{:S(2)}, u32[]{:S(2)}) %collective-permute-start) | collective-permute-done | bytes 20512 | tf_op jit(solution)/shard_map/ppermute | solution.py:64
  89.4 0.1 fusion.11
  89.5 1.5 %collective-permute-start.1 = (f32[4,4,320]{2,1,0:T(4,128)S(1)}, f32[4,4,320]{2,1,0:T(4,128)S(1)}, u32[]{:S(2)}, u32[]{:S(2)}) collective-permute-start(f32[4,4,320]{2,1,0:T(4,128)S(1)} %fusion.11), channel_id=1, source_target_pairs={{0,2},{1,3},{2,0},{3,1},{4,6},{5,7},{6,4},{7,5},{8,10},{9,11},{10,... | collective-permute-start | bytes 61448 | tf_op jit(solution)/shard_map/ppermute | solution.py:64
  91.0 0.4 convolution_multiply_fusion
  91.4 1.0 %copy.26 = bf16[128,2048]{1,0:T(8,128)(2,1)} copy(bf16[128,2048]{0,1:T(8,128)(2,1)S(1)} %bitcast.47) | data formatting | bytes 1048576
  92.4 1.6 %copy.27 = f32[128,3072]{1,0:T(8,128)} copy(f32[128,3072]{0,1:T(8,128)S(1)} %bitcast.46) | data formatting | bytes 3145728
  94.0 0.0 collective-permute-done.1
  94.0 0.1 fusion.25
  94.1 0.1 slice_bitcast_fusion
  94.2 0.7 reshape.112
  94.9 0.6 copy.32
  (8 shorter events, 0.1 us)
Async XLA Ops:
  0.6 23.1 %copy-start = (bf16[4,768]{1,0:T(4,128)(2,1)S(1)}, bf16[4,768]{1,0:T(4,128)(2,1)}, u32[]{:S(2)}) copy-start(bf16[4,768]{1,0:T(4,128)(2,1)} %param.6) | copy-start | bytes 18436
  0.6 50.7 %copy-start.1 = (bf16[128,3072]{1,0:T(8,128)(2,1)S(1)}, bf16[128,3072]{1,0:T(8,128)(2,1)}, u32[]{:S(2)}) copy-start(bf16[128,3072]{1,0:T(8,128)(2,1)} %param.5) | copy-start | bytes 2359300
  0.7 51.0 %copy-start.2 = (s32[128]{0:T(128)S(1)}, s32[128]{0:T(128)}, u32[]{:S(2)}) copy-start(s32[128]{0:T(128)} %param.9) | copy-start | bytes 1540
  52.8 34.0 %copy-start.3 = (u32[32]{0:T(128)S(1)}, u32[32]{0:T(128)}, u32[]{:S(2)}) copy-start(u32[32]{0:T(128)} %constant.50) | copy-start | bytes 388
  88.2 1.2 %collective-permute-start = (f32[4,4,320]{2,1,0:T(4,128)S(1)}, f32[4,4,320]{2,1,0:T(4,128)S(1)}, u32[]{:S(2)}, u32[]{:S(2)}) collective-permute-start(f32[4,4,320]{2,1,0:T(4,128)S(1)} %broadcast_multiply_fusion), channel_id=1, source_target_pairs={{0,1},{1,0},{2,3},{3,2},{4,5},{5,4},{6,7},{7,6},{8,9},{9,8},{10,11... | collective-permute-start | bytes 61448 | tf_op jit(solution)/shard_map/ppermute | solution.py:64
  89.5 4.5 %collective-permute-start.1 = (f32[4,4,320]{2,1,0:T(4,128)S(1)}, f32[4,4,320]{2,1,0:T(4,128)S(1)}, u32[]{:S(2)}, u32[]{:S(2)}) collective-permute-start(f32[4,4,320]{2,1,0:T(4,128)S(1)} %fusion.11), channel_id=1, source_target_pairs={{0,2},{1,3},{2,0},{3,1},{4,6},{5,7},{6,4},{7,5},{8,10},{9,11},{10,... | collective-permute-start | bytes 61448 | tf_op jit(solution)/shard_map/ppermute | solution.py:64
